TPU v7x, 512 devices: a whole 4x4x16 slice. The times are simulated.
512 devices in a mesh: row: 16 (over z), col: 4 (over x_hi, core), depth: 8 (over y, x_lo).
Axes of the slice: x: 4 (x_hi: 2, x_lo: 2; x = x_hi * 2 + x_lo), y: 4, z: 16, core: 2. Of those that a mesh axis runs over, the one named last changes fastest.
Arguments:
- ks_matrix: bfloat16 [4096, 16384], P('col', ('row', 'depth')), may hold values from -6 to 6
- sign_matrix: bfloat16 [16, 8, 128, 12288], P('col', 'depth', None, 'row'), may hold values from -0.046875 to 0.046875
- ks_mask: int32 [32, 128], P('col', ('row', 'depth')), may hold values 0 or 1
- sign_mask: int32 [16, 8, 1, 96], P('col', 'depth', None, 'row'), may hold values 0 or 1
- product_mask: int32 [32, 96], P('col', 'row'), may hold values 0 or 1
- row_order: int32 [4, 8], P('col'), may hold values from 0 to 7, each once within a row
Outputs:
- next_matrix: bfloat16 [4096, 12288], P(('col', 'depth'), 'row')
Inputs may be any that keep to these rules, and one draw needn't show every extreme that they name: Each row of row_order names every number of 0 to 7 once.
All inputs are finite; a program needn't handle non-finite values. No bound on the sum of `ks_mask` or of `sign_mask` or of `product_mask` on one device may be relied on, other than what follows from the above.
Results may differ from a plain program's by a relative error of at most 0.001.
Values may be sent and summed in bfloat16 or wider, within the bound.
No kernel may reach another device: no remote copies, remote signals or barrier semaphores. Data moves between devices by JAX's collectives and lax.ppermute only.
A program may use at most 64 MiB of HBM per device.

v0:
```python
import jax
import jax.numpy as jnp
from jax import lax
from jax.sharding import PartitionSpec as P

BS = 128


def from_behind(block, axis, distance):
    devices = range(lax.axis_size(axis))
    route = [((i - distance) % len(devices), i) for i in devices]
    return lax.ppermute(block, axis, route)


def per_device(ks_matrix, sign_matrix, ks_mask, sign_mask, product_mask, row_order):
    row_blocks, inner_blocks = ks_mask.shape
    local_groups = sign_mask.shape[0]
    sign_inner = sign_mask.shape[2]
    col_blocks = sign_mask.shape[3]
    ks_panel = (
        ks_matrix.reshape(row_blocks, BS, inner_blocks, BS)
        * ks_mask.astype(jnp.bfloat16)[:, None, :, None]
    )
    ks_panel = ks_panel.reshape(row_blocks * BS, inner_blocks * BS)
    sign_kept = sign_matrix.reshape(local_groups, sign_inner, BS, col_blocks, BS)
    sign_kept = sign_kept * sign_mask.astype(jnp.bfloat16).reshape(
        local_groups, sign_inner, 1, col_blocks, 1
    )
    sign_kept = sign_kept.reshape(local_groups, 1, sign_inner * BS, col_blocks * BS)
    sign_whole = lax.all_gather(sign_kept, "col", axis=0, tiled=True)
    row_count = lax.axis_size("row")
    start_sum = jnp.zeros((row_blocks * BS, col_blocks * BS), jnp.float32)
    row_index = lax.axis_index("row")

    def advance(step, carry):
        running, moving = carry
        source = (row_index - step) % row_count
        sign_piece = lax.dynamic_index_in_dim(sign_whole, source, 0, keepdims=False)[0]
        running = running + jnp.dot(moving, sign_piece, preferred_element_type=jnp.float32)
        moving = from_behind(moving, "row", 1)
        return (running, moving)

    running, moving = lax.fori_loop(0, row_count - 1, advance, (start_sum, ks_panel))
    final_source = (row_index - row_count + 1) % row_count
    final_piece = lax.dynamic_index_in_dim(sign_whole, final_source, 0, keepdims=False)[0]
    running = running + jnp.dot(moving, final_piece, preferred_element_type=jnp.float32)
    depth_count = lax.axis_size("depth")
    part_rows = row_blocks // depth_count
    filtered = (
        running.reshape(row_blocks, BS, col_blocks, BS)
        * product_mask.astype(jnp.float32)[:, None, :, None]
    )
    local_order = row_order[0]
    summed = lax.psum(filtered, "depth")
    own_rows = lax.dynamic_slice_in_dim(
        local_order, lax.axis_index("depth") * part_rows, part_rows, 0
    )
    picked = jnp.take(summed, own_rows, axis=0)
    return picked.reshape(part_rows * BS, col_blocks * BS).astype(jnp.bfloat16)


def solution(mesh):
    in_specs = (
        P("col", ("row", "depth")),
        P("col", "depth", None, "row"),
        P("col", ("row", "depth")),
        P("col", "depth", None, "row"),
        P("col", "row"),
        P("col", None),
    )
    out_specs = P(("col", "depth"), "row")
    return jax.shard_map(
        per_device, mesh=mesh, in_specs=in_specs, out_specs=out_specs, check_vma=False
    )
```

profile of v0, /device:TPU:4, one launch (start us, length us, event | category | flops | bytes accessed | tf_op | source)
XLA Modules:
  0.0 356.8 jit_solution(18374426383536028386)
XLA Ops:
  7.3 2.1 broadcast_multiply_fusion.1
  15.4 36.3 %all-gather.2.cloned.1.call-done = bf16[16,1,128,768]{3,2,1,0:T(8,128)(2,1)} async-done(((bf16[4,1,128,768]{3,2,1,0:T(8,128)(2,1)}), bf16[16,1,128,768]{3,2,1,0:T(8,128)(2,1)}) %all-gather.2.cloned.1.call-update) | async-done | bytes 3145744 | tf_op jit(solution)/shard_map/all_gather | solution.py:30
  51.6 171.1 %while.19 = (s32[]{:T(128)}, f32[1024,768]{0,1:T(8,128)S(1)}, bf16[1024,128]{1,0:T(8,128)(2,1)}, s32[]{:T(128)}, bf16[16,1,128,768]{3,2,1,0:T(8,128)(2,1)}, /*index=5*/s32[]{:T(128)}, s32[]{:T(128)}, s32[]{:T(128)}, s32[]{:T(128)}) while((s32[]{:T(128)}, f32[1024,768]{0,1:T(8,128)S(1)}, bf16[1024,128]{1,0:T(8,128)(2,1)}, ...), condition=%wide.region_1.2_spmd.clone, body=%wide.region_0.1_spmd.clone.sunk | while | flops 202899472 | bytes 8323374 | solution.py:43
  52.6 3.7 %collective-permute-start = (bf16[1024,128]{1,0:T(8,128)(2,1)S(1)}, bf16[1024,128]{1,0:T(8,128)(2,1)}, u32[]{:S(2)}, u32[]{:S(2)}) collective-permute-start(bf16[1024,128]{1,0:T(8,128)(2,1)S(1)} %copy.29), channel_id=1, source_target_pairs={{480,0},{0,32},{32,64},{64,96},{96,128},{128,160},{160,192},{192,2... | collective-permute-start | bytes 786440 | tf_op jit(solution)/shard_map/while/body/eval_jaxpr/ppermute | solution.py:12
  56.3 1.9 bitcast_add_fusion.2
  58.2 7.4 %collective-permute-done = bf16[1024,128]{1,0:T(8,128)(2,1)} collective-permute-done((bf16[1024,128]{1,0:T(8,128)(2,1)S(1)}, bf16[1024,128]{1,0:T(8,128)(2,1)}, u32[]{:S(2)}, u32[]{:S(2)}) %collective-permute-start) | collective-permute-done | bytes 262176 | tf_op jit(solution)/shard_map/while/body/eval_jaxpr/ppermute | solution.py:12
  66.5 1.9 collective-permute-start
  68.5 1.9 bitcast_add_fusion.2
  70.3 7.3 %collective-permute-done = bf16[1024,128]{1,0:T(8,128)(2,1)} collective-permute-done((bf16[1024,128]{1,0:T(8,128)(2,1)S(1)}, bf16[1024,128]{1,0:T(8,128)(2,1)}, u32[]{:S(2)}, u32[]{:S(2)}) %collective-permute-start) | collective-permute-done | bytes 262176 | tf_op jit(solution)/shard_map/while/body/eval_jaxpr/ppermute | solution.py:12
  78.6 1.9 collective-permute-start
  82.4 6.5 %collective-permute-done = bf16[1024,128]{1,0:T(8,128)(2,1)} collective-permute-done((bf16[1024,128]{1,0:T(8,128)(2,1)S(1)}, bf16[1024,128]{1,0:T(8,128)(2,1)}, u32[]{:S(2)}, u32[]{:S(2)}) %collective-permute-start) | collective-permute-done | bytes 262176 | tf_op jit(solution)/shard_map/while/body/eval_jaxpr/ppermute | solution.py:12
  89.9 1.9 collective-permute-start
  91.8 1.9 bitcast_add_fusion.2
  93.7 5.7 %collective-permute-done = bf16[1024,128]{1,0:T(8,128)(2,1)} collective-permute-done((bf16[1024,128]{1,0:T(8,128)(2,1)S(1)}, bf16[1024,128]{1,0:T(8,128)(2,1)}, u32[]{:S(2)}, u32[]{:S(2)}) %collective-permute-start) | collective-permute-done | bytes 262176 | tf_op jit(solution)/shard_map/while/body/eval_jaxpr/ppermute | solution.py:12
  100.4 1.9 collective-permute-start
  104.2 5.7 %collective-permute-done = bf16[1024,128]{1,0:T(8,128)(2,1)} collective-permute-done((bf16[1024,128]{1,0:T(8,128)(2,1)S(1)}, bf16[1024,128]{1,0:T(8,128)(2,1)}, u32[]{:S(2)}, u32[]{:S(2)}) %collective-permute-start) | collective-permute-done | bytes 262176 | tf_op jit(solution)/shard_map/while/body/eval_jaxpr/ppermute | solution.py:12
  110.9 1.9 collective-permute-start
  114.7 5.7 %collective-permute-done = bf16[1024,128]{1,0:T(8,128)(2,1)} collective-permute-done((bf16[1024,128]{1,0:T(8,128)(2,1)S(1)}, bf16[1024,128]{1,0:T(8,128)(2,1)}, u32[]{:S(2)}, u32[]{:S(2)}) %collective-permute-start) | collective-permute-done | bytes 262176 | tf_op jit(solution)/shard_map/while/body/eval_jaxpr/ppermute | solution.py:12
  121.4 1.9 collective-permute-start
  125.2 5.7 %collective-permute-done = bf16[1024,128]{1,0:T(8,128)(2,1)} collective-permute-done((bf16[1024,128]{1,0:T(8,128)(2,1)S(1)}, bf16[1024,128]{1,0:T(8,128)(2,1)}, u32[]{:S(2)}, u32[]{:S(2)}) %collective-permute-start) | collective-permute-done | bytes 262176 | tf_op jit(solution)/shard_map/while/body/eval_jaxpr/ppermute | solution.py:12
  131.9 1.9 collective-permute-start
  133.9 1.9 bitcast_add_fusion.2
  135.8 6.7 %collective-permute-done = bf16[1024,128]{1,0:T(8,128)(2,1)} collective-permute-done((bf16[1024,128]{1,0:T(8,128)(2,1)S(1)}, bf16[1024,128]{1,0:T(8,128)(2,1)}, u32[]{:S(2)}, u32[]{:S(2)}) %collective-permute-start) | collective-permute-done | bytes 262176 | tf_op jit(solution)/shard_map/while/body/eval_jaxpr/ppermute | solution.py:12
  143.5 1.9 collective-permute-start
  145.4 1.9 bitcast_add_fusion.2
  147.3 7.9 %collective-permute-done = bf16[1024,128]{1,0:T(8,128)(2,1)} collective-permute-done((bf16[1024,128]{1,0:T(8,128)(2,1)S(1)}, bf16[1024,128]{1,0:T(8,128)(2,1)}, u32[]{:S(2)}, u32[]{:S(2)}) %collective-permute-start) | collective-permute-done | bytes 262176 | tf_op jit(solution)/shard_map/while/body/eval_jaxpr/ppermute | solution.py:12
  156.2 1.9 collective-permute-start
  158.1 1.9 bitcast_add_fusion.2
  160.0 8.0 %collective-permute-done = bf16[1024,128]{1,0:T(8,128)(2,1)} collective-permute-done((bf16[1024,128]{1,0:T(8,128)(2,1)S(1)}, bf16[1024,128]{1,0:T(8,128)(2,1)}, u32[]{:S(2)}, u32[]{:S(2)}) %collective-permute-start) | collective-permute-done | bytes 262176 | tf_op jit(solution)/shard_map/while/body/eval_jaxpr/ppermute | solution.py:12
  169.0 1.9 collective-permute-start
  172.8 7.2 %collective-permute-done = bf16[1024,128]{1,0:T(8,128)(2,1)} collective-permute-done((bf16[1024,128]{1,0:T(8,128)(2,1)S(1)}, bf16[1024,128]{1,0:T(8,128)(2,1)}, u32[]{:S(2)}, u32[]{:S(2)}) %collective-permute-start) | collective-permute-done | bytes 262176 | tf_op jit(solution)/shard_map/while/body/eval_jaxpr/ppermute | solution.py:12
  181.0 1.9 collective-permute-start
  182.9 1.9 bitcast_add_fusion.2
  184.8 6.3 %collective-permute-done = bf16[1024,128]{1,0:T(8,128)(2,1)} collective-permute-done((bf16[1024,128]{1,0:T(8,128)(2,1)S(1)}, bf16[1024,128]{1,0:T(8,128)(2,1)}, u32[]{:S(2)}, u32[]{:S(2)}) %collective-permute-start) | collective-permute-done | bytes 262176 | tf_op jit(solution)/shard_map/while/body/eval_jaxpr/ppermute | solution.py:12
  192.1 1.9 collective-permute-start
  194.0 1.9 bitcast_add_fusion.2
  195.9 5.7 %collective-permute-done = bf16[1024,128]{1,0:T(8,128)(2,1)} collective-permute-done((bf16[1024,128]{1,0:T(8,128)(2,1)S(1)}, bf16[1024,128]{1,0:T(8,128)(2,1)}, u32[]{:S(2)}, u32[]{:S(2)}) %collective-permute-start) | collective-permute-done | bytes 262176 | tf_op jit(solution)/shard_map/while/body/eval_jaxpr/ppermute | solution.py:12
  202.6 1.9 collective-permute-start
  206.4 5.7 %collective-permute-done = bf16[1024,128]{1,0:T(8,128)(2,1)} collective-permute-done((bf16[1024,128]{1,0:T(8,128)(2,1)S(1)}, bf16[1024,128]{1,0:T(8,128)(2,1)}, u32[]{:S(2)}, u32[]{:S(2)}) %collective-permute-start) | collective-permute-done | bytes 262176 | tf_op jit(solution)/shard_map/while/body/eval_jaxpr/ppermute | solution.py:12
  213.1 1.9 collective-permute-start
  215.1 1.9 bitcast_add_fusion.2
  217.0 5.7 %collective-permute-done = bf16[1024,128]{1,0:T(8,128)(2,1)} collective-permute-done((bf16[1024,128]{1,0:T(8,128)(2,1)S(1)}, bf16[1024,128]{1,0:T(8,128)(2,1)}, u32[]{:S(2)}, u32[]{:S(2)}) %collective-permute-start) | collective-permute-done | bytes 262176 | tf_op jit(solution)/shard_map/while/body/eval_jaxpr/ppermute | solution.py:12
  222.7 2.4 copy.12
  225.1 2.6 convolution_add_fusion
  227.7 2.3 copy.13
  230.0 2.6 copy.19
  233.0 114.2 %all-reduce.1 = bf16[8,128,6,128]{1,0,3,2:T(8,128)(2,1)} all-reduce(f32[8,128,6,128]{1,0,3,2:T(8,128)S(1)} %broadcast_multiply_fusion), channel_id=1, replica_groups=mesh['row'=16,'col'=4,'depth'=8] {'depth'}, use_global_device_ids=true, to_apply=%region_2.3 | all-reduce | flops 786432 | bytes 4718592 | tf_op jit(solution)/shard_map/psum | solution.py:54
  347.1 1.9 fusion.3
  (39 shorter events, 31.4 us)
Async XLA Ops:
  6.5 3.7 %copy-start = (s32[1,8]{1,0:T(1,128)S(1)}, s32[1,8]{1,0:T(1,128)}, u32[]{:S(2)}) copy-start(s32[1,8]{1,0:T(1,128)} %param.13) | copy-start | bytes 100
  6.5 45.1 %all-gather.2.cloned.1.call-start = ((), (), s32[]{:S(2)}) async-start(), calls=%async_computation | async-start | bytes 3932160 | tf_op jit(solution)/shard_map/all_gather | solution.py:30
  52.6 13.0 %collective-permute-start = (bf16[1024,128]{1,0:T(8,128)(2,1)S(1)}, bf16[1024,128]{1,0:T(8,128)(2,1)}, u32[]{:S(2)}, u32[]{:S(2)}) collective-permute-start(bf16[1024,128]{1,0:T(8,128)(2,1)S(1)} %copy.29), channel_id=1, source_target_pairs={{480,0},{0,32},{32,64},{64,96},{96,128},{128,160},{160,192},{192,2... | collective-permute-start | bytes 786440 | tf_op jit(solution)/shard_map/while/body/eval_jaxpr/ppermute | solution.py:12
  66.5 11.2 %collective-permute-start = (bf16[1024,128]{1,0:T(8,128)(2,1)S(1)}, bf16[1024,128]{1,0:T(8,128)(2,1)}, u32[]{:S(2)}, u32[]{:S(2)}) collective-permute-start(bf16[1024,128]{1,0:T(8,128)(2,1)S(1)} %copy.29), channel_id=1, source_target_pairs={{480,0},{0,32},{32,64},{64,96},{96,128},{128,160},{160,192},{192,2... | collective-permute-start | bytes 786440 | tf_op jit(solution)/shard_map/while/body/eval_jaxpr/ppermute | solution.py:12
  78.6 10.3 %collective-permute-start = (bf16[1024,128]{1,0:T(8,128)(2,1)S(1)}, bf16[1024,128]{1,0:T(8,128)(2,1)}, u32[]{:S(2)}, u32[]{:S(2)}) collective-permute-start(bf16[1024,128]{1,0:T(8,128)(2,1)S(1)} %copy.29), channel_id=1, source_target_pairs={{480,0},{0,32},{32,64},{64,96},{96,128},{128,160},{160,192},{192,2... | collective-permute-start | bytes 786440 | tf_op jit(solution)/shard_map/while/body/eval_jaxpr/ppermute | solution.py:12
  89.9 9.6 %collective-permute-start = (bf16[1024,128]{1,0:T(8,128)(2,1)S(1)}, bf16[1024,128]{1,0:T(8,128)(2,1)}, u32[]{:S(2)}, u32[]{:S(2)}) collective-permute-start(bf16[1024,128]{1,0:T(8,128)(2,1)S(1)} %copy.29), channel_id=1, source_target_pairs={{480,0},{0,32},{32,64},{64,96},{96,128},{128,160},{160,192},{192,2... | collective-permute-start | bytes 786440 | tf_op jit(solution)/shard_map/while/body/eval_jaxpr/ppermute | solution.py:12
  100.4 9.6 %collective-permute-start = (bf16[1024,128]{1,0:T(8,128)(2,1)S(1)}, bf16[1024,128]{1,0:T(8,128)(2,1)}, u32[]{:S(2)}, u32[]{:S(2)}) collective-permute-start(bf16[1024,128]{1,0:T(8,128)(2,1)S(1)} %copy.29), channel_id=1, source_target_pairs={{480,0},{0,32},{32,64},{64,96},{96,128},{128,160},{160,192},{192,2... | collective-permute-start | bytes 786440 | tf_op jit(solution)/shard_map/while/body/eval_jaxpr/ppermute | solution.py:12
  110.9 9.6 %collective-permute-start = (bf16[1024,128]{1,0:T(8,128)(2,1)S(1)}, bf16[1024,128]{1,0:T(8,128)(2,1)}, u32[]{:S(2)}, u32[]{:S(2)}) collective-permute-start(bf16[1024,128]{1,0:T(8,128)(2,1)S(1)} %copy.29), channel_id=1, source_target_pairs={{480,0},{0,32},{32,64},{64,96},{96,128},{128,160},{160,192},{192,2... | collective-permute-start | bytes 786440 | tf_op jit(solution)/shard_map/while/body/eval_jaxpr/ppermute | solution.py:12
  121.4 9.6 %collective-permute-start = (bf16[1024,128]{1,0:T(8,128)(2,1)S(1)}, bf16[1024,128]{1,0:T(8,128)(2,1)}, u32[]{:S(2)}, u32[]{:S(2)}) collective-permute-start(bf16[1024,128]{1,0:T(8,128)(2,1)S(1)} %copy.29), channel_id=1, source_target_pairs={{480,0},{0,32},{32,64},{64,96},{96,128},{128,160},{160,192},{192,2... | collective-permute-start | bytes 786440 | tf_op jit(solution)/shard_map/while/body/eval_jaxpr/ppermute | solution.py:12
  131.9 10.6 %collective-permute-start = (bf16[1024,128]{1,0:T(8,128)(2,1)S(1)}, bf16[1024,128]{1,0:T(8,128)(2,1)}, u32[]{:S(2)}, u32[]{:S(2)}) collective-permute-start(bf16[1024,128]{1,0:T(8,128)(2,1)S(1)} %copy.29), channel_id=1, source_target_pairs={{480,0},{0,32},{32,64},{64,96},{96,128},{128,160},{160,192},{192,2... | collective-permute-start | bytes 786440 | tf_op jit(solution)/shard_map/while/body/eval_jaxpr/ppermute | solution.py:12
  143.5 11.8 %collective-permute-start = (bf16[1024,128]{1,0:T(8,128)(2,1)S(1)}, bf16[1024,128]{1,0:T(8,128)(2,1)}, u32[]{:S(2)}, u32[]{:S(2)}) collective-permute-start(bf16[1024,128]{1,0:T(8,128)(2,1)S(1)} %copy.29), channel_id=1, source_target_pairs={{480,0},{0,32},{32,64},{64,96},{96,128},{128,160},{160,192},{192,2... | collective-permute-start | bytes 786440 | tf_op jit(solution)/shard_map/while/body/eval_jaxpr/ppermute | solution.py:12
  156.2 11.8 %collective-permute-start = (bf16[1024,128]{1,0:T(8,128)(2,1)S(1)}, bf16[1024,128]{1,0:T(8,128)(2,1)}, u32[]{:S(2)}, u32[]{:S(2)}) collective-permute-start(bf16[1024,128]{1,0:T(8,128)(2,1)S(1)} %copy.29), channel_id=1, source_target_pairs={{480,0},{0,32},{32,64},{64,96},{96,128},{128,160},{160,192},{192,2... | collective-permute-start | bytes 786440 | tf_op jit(solution)/shard_map/while/body/eval_jaxpr/ppermute | solution.py:12
  169.0 11.1 %collective-permute-start = (bf16[1024,128]{1,0:T(8,128)(2,1)S(1)}, bf16[1024,128]{1,0:T(8,128)(2,1)}, u32[]{:S(2)}, u32[]{:S(2)}) collective-permute-start(bf16[1024,128]{1,0:T(8,128)(2,1)S(1)} %copy.29), channel_id=1, source_target_pairs={{480,0},{0,32},{32,64},{64,96},{96,128},{128,160},{160,192},{192,2... | collective-permute-start | bytes 786440 | tf_op jit(solution)/shard_map/while/body/eval_jaxpr/ppermute | solution.py:12
  181.0 10.2 %collective-permute-start = (bf16[1024,128]{1,0:T(8,128)(2,1)S(1)}, bf16[1024,128]{1,0:T(8,128)(2,1)}, u32[]{:S(2)}, u32[]{:S(2)}) collective-permute-start(bf16[1024,128]{1,0:T(8,128)(2,1)S(1)} %copy.29), channel_id=1, source_target_pairs={{480,0},{0,32},{32,64},{64,96},{96,128},{128,160},{160,192},{192,2... | collective-permute-start | bytes 786440 | tf_op jit(solution)/shard_map/while/body/eval_jaxpr/ppermute | solution.py:12
  192.1 9.6 %collective-permute-start = (bf16[1024,128]{1,0:T(8,128)(2,1)S(1)}, bf16[1024,128]{1,0:T(8,128)(2,1)}, u32[]{:S(2)}, u32[]{:S(2)}) collective-permute-start(bf16[1024,128]{1,0:T(8,128)(2,1)S(1)} %copy.29), channel_id=1, source_target_pairs={{480,0},{0,32},{32,64},{64,96},{96,128},{128,160},{160,192},{192,2... | collective-permute-start | bytes 786440 | tf_op jit(solution)/shard_map/while/body/eval_jaxpr/ppermute | solution.py:12
  202.6 9.6 %collective-permute-start = (bf16[1024,128]{1,0:T(8,128)(2,1)S(1)}, bf16[1024,128]{1,0:T(8,128)(2,1)}, u32[]{:S(2)}, u32[]{:S(2)}) collective-permute-start(bf16[1024,128]{1,0:T(8,128)(2,1)S(1)} %copy.29), channel_id=1, source_target_pairs={{480,0},{0,32},{32,64},{64,96},{96,128},{128,160},{160,192},{192,2... | collective-permute-start | bytes 786440 | tf_op jit(solution)/shard_map/while/body/eval_jaxpr/ppermute | solution.py:12
  213.1 9.6 %collective-permute-start = (bf16[1024,128]{1,0:T(8,128)(2,1)S(1)}, bf16[1024,128]{1,0:T(8,128)(2,1)}, u32[]{:S(2)}, u32[]{:S(2)}) collective-permute-start(bf16[1024,128]{1,0:T(8,128)(2,1)S(1)} %copy.29), channel_id=1, source_target_pairs={{480,0},{0,32},{32,64},{64,96},{96,128},{128,160},{160,192},{192,2... | collective-permute-start | bytes 786440 | tf_op jit(solution)/shard_map/while/body/eval_jaxpr/ppermute | solution.py:12
Sparse Core Ops, SparseCore 0:
  9.5 42.0 all-gather.1
where the time goes:
time: 358 us; the launch traced here: 357 us
  waiting for transfers between devices  134 us (37%)
  blocking collectives  114 us (32%)
  matrix products  30.7 us (9%)
  starting transfers between devices  30.4 us (8%)
  local copies, waits for them, and re-layouts  23.3 us (7%)
  between operations  15.4 us (4%)
  other arithmetic  8.19 us (2%)
    psum x1, blocking collectives, per_device(): summed = lax.psum(filtered, 'depth')  114 us
    ppermute x15, waiting for transfers between devices, from_behind(): return lax.ppermute(block, axis, route)  97.7 us
    all_gather x1, waiting for transfers between devices, per_device(): sign_whole = lax.all_gather(sign_kept, 'col', axis=0, tiled=True)  36.3 us
    ppermute x15, starting transfers between devices, from_behind(): return lax.ppermute(block, axis, route)  30.4 us
    dot_general x15, matrix products, advance(): jnp.dot(moving, sign_piece, preferred_element_type=jnp.float32)  28.1 us
    while x15, local copies, waits for them, and re-layouts  14.3 us
  transfers between devices with their start and end apart: 16, of which 16 were waited for; matrix products, arithmetic and copies ran while one was open for 9% of the time, Pallas kernels for 0%

commit v1 on v0

--- a/solution.py
+++ b/solution.py
@@ -51,7 +51,7 @@
         * product_mask.astype(jnp.float32)[:, None, :, None]
     )
     local_order = row_order[0]
-    summed = lax.psum(filtered, "depth")
+    summed = jnp.sum(lax.all_gather(filtered, "depth"), axis=0)
     own_rows = lax.dynamic_slice_in_dim(
         local_order, lax.axis_index("depth") * part_rows, part_rows, 0
     )

time: 358 us -> 747 us (2.09)
  the two profiles are of different devices: /device:TPU:4 before, /device:TPU:1 now
where the time goes in v1:
time: 747 us; the launch traced here: 745 us
  waiting for transfers between devices  626 us (84%)
  matrix products  30.7 us (4%)
  starting transfers between devices  29.9 us (4%)
  local copies, waits for them, and re-layouts  26.2 us (4%)
  other arithmetic  16.3 us (2%)
  between operations  15.5 us (2%)
    all_gather x1, waiting for transfers between devices, per_device(): summed = jnp.sum(lax.all_gather(filtered, 'depth'), axis=0)  501 us
    ppermute x15, waiting for transfers between devices, from_behind(): return lax.ppermute(block, axis, route)  82.7 us
    all_gather x1, waiting for transfers between devices, per_device(): sign_whole = lax.all_gather(sign_kept, 'col', axis=0, tiled=True)  42.7 us
    ppermute x15, starting transfers between devices, from_behind(): return lax.ppermute(block, axis, route)  29.9 us
    dot_general x15, matrix products, advance(): jnp.dot(moving, sign_piece, preferred_element_type=jnp.float32)  28.1 us
  transfers between devices with their start and end apart: 17, of which 17 were waited for; matrix products, arithmetic and copies ran while one was open for 4% of the time, Pallas kernels for 0%

profile of v1, /device:TPU:1, one launch (start us, length us, event | category | flops | bytes accessed | tf_op | source)
XLA Modules:
  0.0 745.1 jit_solution(13880398359097400717)
XLA Ops:
  7.3 2.1 broadcast_multiply_fusion.1
  12.9 42.7 %all-gather.3.cloned.1.call-done = bf16[16,1,128,768]{3,2,1,0:T(8,128)(2,1)} async-done(((bf16[4,1,128,768]{3,2,1,0:T(8,128)(2,1)}), bf16[16,1,128,768]{3,2,1,0:T(8,128)(2,1)}) %all-gather.3.cloned.1.call-update) | async-done | bytes 3145744 | tf_op jit(solution)/shard_map/all_gather | solution.py:30
  55.5 155.6 %while.19 = (s32[]{:T(128)}, f32[1024,768]{0,1:T(8,128)S(1)}, bf16[1024,128]{1,0:T(8,128)(2,1)}, s32[]{:T(128)}, bf16[16,1,128,768]{3,2,1,0:T(8,128)(2,1)}, /*index=5*/s32[]{:T(128)}, s32[]{:T(128)}, s32[]{:T(128)}, s32[]{:T(128)}) while((s32[]{:T(128)}, f32[1024,768]{0,1:T(8,128)S(1)}, bf16[1024,128]{1,0:T(8,128)(2,1)}, ...), condition=%wide.region_1.2_spmd.clone, body=%wide.region_0.1_spmd.clone.sunk | while | flops 202899472 | bytes 8323374 | solution.py:43
  56.5 3.2 collective-permute-start
  61.6 7.2 collective-permute-done
  69.7 1.9 collective-permute-start
  71.6 1.9 bitcast_add_fusion.2
  73.5 6.4 collective-permute-done
  80.9 1.9 collective-permute-start
  82.9 1.9 bitcast_add_fusion.2
  84.8 5.5 collective-permute-done
  91.2 1.9 collective-permute-start
  93.2 1.9 bitcast_add_fusion.2
  95.1 4.6 collective-permute-done
  100.6 1.9 collective-permute-start
  102.5 1.9 bitcast_add_fusion.2
  104.4 4.6 collective-permute-done
  110.0 1.9 collective-permute-start
  113.8 4.6 collective-permute-done
  119.3 1.9 collective-permute-start
  121.3 1.9 bitcast_add_fusion.2
  123.2 4.6 collective-permute-done
  128.7 1.9 collective-permute-start
  130.7 1.9 bitcast_add_fusion.2
  132.5 4.6 collective-permute-done
  138.1 1.9 collective-permute-start
  140.0 1.9 bitcast_add_fusion.2
  141.9 5.7 collective-permute-done
  148.5 1.9 collective-permute-start
  152.3 6.7 collective-permute-done
  160.0 1.9 collective-permute-start
  163.9 7.2 collective-permute-done
  172.1 1.9 collective-permute-start
  175.9 6.3 collective-permute-done
  183.2 1.9 collective-permute-start
  187.0 5.4 collective-permute-done
  193.3 1.9 collective-permute-start
  197.2 4.6 collective-permute-done
  202.7 1.9 collective-permute-start
  204.7 1.9 bitcast_add_fusion.2
  206.5 4.6 collective-permute-done
  211.1 2.4 copy.12
  213.5 2.6 convolution_add_fusion
  216.2 2.4 copy.13
  218.5 2.6 copy.23
  221.5 2.4 copy.15
  226.5 500.5 %all-gather.5.cloned.1.call-done = f32[8,8,128,6,128]{4,2,3,1,0:T(8,128)} async-done(((f32[1,8,128,6,128]{4,2,3,1,0:T(8,128)}), f32[8,8,128,6,128]{4,2,3,1,0:T(8,128)}) %all-gather.5.cloned.1.call-update) | async-done | bytes 25165840 | tf_op jit(solution)/shard_map/all_gather | solution.py:54
  727.0 9.6 %reduce_sum.9 = bf16[8,128,6,128]{3,1,2,0:T(8,128)(2,1)S(1)} reduce(f32[8,8,128,6,128]{4,2,3,1,0:T(8,128)} %all-gather.5.cloned.1.call-done, f32[]{:T(128)} %constant.92.clone.1), dimensions={0}, to_apply=%region_2.3 | reduce | flops 5505024 | bytes 26738692 | tf_op jit(solution)/shard_map/reduce_sum | solution.py:54
  (45 shorter events, 34.1 us)
Async XLA Ops:
  6.5 217.4 %copy-start = (s32[1,8]{1,0:T(1,128)S(1)}, s32[1,8]{1,0:T(1,128)}, u32[]{:S(2)}) copy-start(s32[1,8]{1,0:T(1,128)} %param.13) | copy-start | bytes 100
  6.5 49.0 %all-gather.3.cloned.1.call-start = ((), (), s32[]{:S(2)}) async-start(), calls=%async_computation | async-start | bytes 3932160 | tf_op jit(solution)/shard_map/all_gather | solution.py:30
  9.4 717.5 %all-gather.5.cloned.1.call-start = ((), (), s32[]{:S(2)}) async-start(), calls=%async_computation.1 | async-start | bytes 28311552 | tf_op jit(solution)/shard_map/all_gather | solution.py:54
  56.5 12.3 %collective-permute-start = (bf16[1024,128]{1,0:T(8,128)(2,1)S(1)}, bf16[1024,128]{1,0:T(8,128)(2,1)}, u32[]{:S(2)}, u32[]{:S(2)}) collective-permute-start(bf16[1024,128]{1,0:T(8,128)(2,1)S(1)} %copy.33), channel_id=1, source_target_pairs={{480,0},{0,32},{32,64},{64,96},{96,128},{128,160},{160,192},{192,2... | collective-permute-start | bytes 786440 | tf_op jit(solution)/shard_map/while/body/eval_jaxpr/ppermute | solution.py:12
  69.7 10.3 %collective-permute-start = (bf16[1024,128]{1,0:T(8,128)(2,1)S(1)}, bf16[1024,128]{1,0:T(8,128)(2,1)}, u32[]{:S(2)}, u32[]{:S(2)}) collective-permute-start(bf16[1024,128]{1,0:T(8,128)(2,1)S(1)} %copy.33), channel_id=1, source_target_pairs={{480,0},{0,32},{32,64},{64,96},{96,128},{128,160},{160,192},{192,2... | collective-permute-start | bytes 786440 | tf_op jit(solution)/shard_map/while/body/eval_jaxpr/ppermute | solution.py:12
  80.9 9.4 %collective-permute-start = (bf16[1024,128]{1,0:T(8,128)(2,1)S(1)}, bf16[1024,128]{1,0:T(8,128)(2,1)}, u32[]{:S(2)}, u32[]{:S(2)}) collective-permute-start(bf16[1024,128]{1,0:T(8,128)(2,1)S(1)} %copy.33), channel_id=1, source_target_pairs={{480,0},{0,32},{32,64},{64,96},{96,128},{128,160},{160,192},{192,2... | collective-permute-start | bytes 786440 | tf_op jit(solution)/shard_map/while/body/eval_jaxpr/ppermute | solution.py:12
  91.2 8.4 %collective-permute-start = (bf16[1024,128]{1,0:T(8,128)(2,1)S(1)}, bf16[1024,128]{1,0:T(8,128)(2,1)}, u32[]{:S(2)}, u32[]{:S(2)}) collective-permute-start(bf16[1024,128]{1,0:T(8,128)(2,1)S(1)} %copy.33), channel_id=1, source_target_pairs={{480,0},{0,32},{32,64},{64,96},{96,128},{128,160},{160,192},{192,2... | collective-permute-start | bytes 786440 | tf_op jit(solution)/shard_map/while/body/eval_jaxpr/ppermute | solution.py:12
  100.6 8.4 %collective-permute-start = (bf16[1024,128]{1,0:T(8,128)(2,1)S(1)}, bf16[1024,128]{1,0:T(8,128)(2,1)}, u32[]{:S(2)}, u32[]{:S(2)}) collective-permute-start(bf16[1024,128]{1,0:T(8,128)(2,1)S(1)} %copy.33), channel_id=1, source_target_pairs={{480,0},{0,32},{32,64},{64,96},{96,128},{128,160},{160,192},{192,2... | collective-permute-start | bytes 786440 | tf_op jit(solution)/shard_map/while/body/eval_jaxpr/ppermute | solution.py:12
  110.0 8.4 %collective-permute-start = (bf16[1024,128]{1,0:T(8,128)(2,1)S(1)}, bf16[1024,128]{1,0:T(8,128)(2,1)}, u32[]{:S(2)}, u32[]{:S(2)}) collective-permute-start(bf16[1024,128]{1,0:T(8,128)(2,1)S(1)} %copy.33), channel_id=1, source_target_pairs={{480,0},{0,32},{32,64},{64,96},{96,128},{128,160},{160,192},{192,2... | collective-permute-start | bytes 786440 | tf_op jit(solution)/shard_map/while/body/eval_jaxpr/ppermute | solution.py:12
  119.3 8.4 %collective-permute-start = (bf16[1024,128]{1,0:T(8,128)(2,1)S(1)}, bf16[1024,128]{1,0:T(8,128)(2,1)}, u32[]{:S(2)}, u32[]{:S(2)}) collective-permute-start(bf16[1024,128]{1,0:T(8,128)(2,1)S(1)} %copy.33), channel_id=1, source_target_pairs={{480,0},{0,32},{32,64},{64,96},{96,128},{128,160},{160,192},{192,2... | collective-permute-start | bytes 786440 | tf_op jit(solution)/shard_map/while/body/eval_jaxpr/ppermute | solution.py:12
  128.7 8.4 %collective-permute-start = (bf16[1024,128]{1,0:T(8,128)(2,1)S(1)}, bf16[1024,128]{1,0:T(8,128)(2,1)}, u32[]{:S(2)}, u32[]{:S(2)}) collective-permute-start(bf16[1024,128]{1,0:T(8,128)(2,1)S(1)} %copy.33), channel_id=1, source_target_pairs={{480,0},{0,32},{32,64},{64,96},{96,128},{128,160},{160,192},{192,2... | collective-permute-start | bytes 786440 | tf_op jit(solution)/shard_map/while/body/eval_jaxpr/ppermute | solution.py:12
  138.1 9.5 %collective-permute-start = (bf16[1024,128]{1,0:T(8,128)(2,1)S(1)}, bf16[1024,128]{1,0:T(8,128)(2,1)}, u32[]{:S(2)}, u32[]{:S(2)}) collective-permute-start(bf16[1024,128]{1,0:T(8,128)(2,1)S(1)} %copy.33), channel_id=1, source_target_pairs={{480,0},{0,32},{32,64},{64,96},{96,128},{128,160},{160,192},{192,2... | collective-permute-start | bytes 786440 | tf_op jit(solution)/shard_map/while/body/eval_jaxpr/ppermute | solution.py:12
  148.5 10.6 %collective-permute-start = (bf16[1024,128]{1,0:T(8,128)(2,1)S(1)}, bf16[1024,128]{1,0:T(8,128)(2,1)}, u32[]{:S(2)}, u32[]{:S(2)}) collective-permute-start(bf16[1024,128]{1,0:T(8,128)(2,1)S(1)} %copy.33), channel_id=1, source_target_pairs={{480,0},{0,32},{32,64},{64,96},{96,128},{128,160},{160,192},{192,2... | collective-permute-start | bytes 786440 | tf_op jit(solution)/shard_map/while/body/eval_jaxpr/ppermute | solution.py:12
  160.0 11.1 %collective-permute-start = (bf16[1024,128]{1,0:T(8,128)(2,1)S(1)}, bf16[1024,128]{1,0:T(8,128)(2,1)}, u32[]{:S(2)}, u32[]{:S(2)}) collective-permute-start(bf16[1024,128]{1,0:T(8,128)(2,1)S(1)} %copy.33), channel_id=1, source_target_pairs={{480,0},{0,32},{32,64},{64,96},{96,128},{128,160},{160,192},{192,2... | collective-permute-start | bytes 786440 | tf_op jit(solution)/shard_map/while/body/eval_jaxpr/ppermute | solution.py:12
  172.1 10.2 %collective-permute-start = (bf16[1024,128]{1,0:T(8,128)(2,1)S(1)}, bf16[1024,128]{1,0:T(8,128)(2,1)}, u32[]{:S(2)}, u32[]{:S(2)}) collective-permute-start(bf16[1024,128]{1,0:T(8,128)(2,1)S(1)} %copy.33), channel_id=1, source_target_pairs={{480,0},{0,32},{32,64},{64,96},{96,128},{128,160},{160,192},{192,2... | collective-permute-start | bytes 786440 | tf_op jit(solution)/shard_map/while/body/eval_jaxpr/ppermute | solution.py:12
  183.2 9.2 %collective-permute-start = (bf16[1024,128]{1,0:T(8,128)(2,1)S(1)}, bf16[1024,128]{1,0:T(8,128)(2,1)}, u32[]{:S(2)}, u32[]{:S(2)}) collective-permute-start(bf16[1024,128]{1,0:T(8,128)(2,1)S(1)} %copy.33), channel_id=1, source_target_pairs={{480,0},{0,32},{32,64},{64,96},{96,128},{128,160},{160,192},{192,2... | collective-permute-start | bytes 786440 | tf_op jit(solution)/shard_map/while/body/eval_jaxpr/ppermute | solution.py:12
  193.3 8.4 %collective-permute-start = (bf16[1024,128]{1,0:T(8,128)(2,1)S(1)}, bf16[1024,128]{1,0:T(8,128)(2,1)}, u32[]{:S(2)}, u32[]{:S(2)}) collective-permute-start(bf16[1024,128]{1,0:T(8,128)(2,1)S(1)} %copy.33), channel_id=1, source_target_pairs={{480,0},{0,32},{32,64},{64,96},{96,128},{128,160},{160,192},{192,2... | collective-permute-start | bytes 786440 | tf_op jit(solution)/shard_map/while/body/eval_jaxpr/ppermute | solution.py:12
  202.7 8.4 %collective-permute-start = (bf16[1024,128]{1,0:T(8,128)(2,1)S(1)}, bf16[1024,128]{1,0:T(8,128)(2,1)}, u32[]{:S(2)}, u32[]{:S(2)}) collective-permute-start(bf16[1024,128]{1,0:T(8,128)(2,1)S(1)} %copy.33), channel_id=1, source_target_pairs={{480,0},{0,32},{32,64},{64,96},{96,128},{128,160},{160,192},{192,2... | collective-permute-start | bytes 786440 | tf_op jit(solution)/shard_map/while/body/eval_jaxpr/ppermute | solution.py:12
Sparse Core Ops, SparseCore 0:
  9.5 45.9 all-gather.2
  224.0 502.8 all-gather.4
